TPU v7x, 32 devices: a whole 2x2x4 slice. The times are simulated.
32 devices in a mesh: node: 8 (over z, x), feat: 4 (over y, core).
Axes of the slice: x: 2, y: 2, z: 4, core: 2. Of those that a mesh axis runs over, the one named last changes fastest.
Arguments:
- features: bfloat16 [128, 128, 128], P('node', 'feat'), may hold values from -6 to 6
- tile_values: bfloat16 [2048, 128, 128], P('node'), may hold values from -0.125 to 0.125
- tile_row: int32 [2048], P('node'), may hold values from 0 to 127, as said below
- tile_col: int32 [2048], P('node'), may hold values from 0 to 127, as said below
- tile_count: int32 [8], P('node'), may hold values from 32 to 256, as said below
- weight: float32 [128, 128], P('feat'), may hold values from -0.5 to 0.5
- first_moment: float32 [128, 128], P('feat'), may hold values from -3 to 3
- second_moment: float32 [128, 128], P('feat'), may hold values from 0.1 to 2
- cotangent: bfloat16 [128, 128, 128], P('node', 'feat'), may hold values from -6 to 6
Outputs:
- activated: bfloat16 [128, 128, 128], P('node', 'feat')
- feature_grad: float32 [128, 128, 128], P('node', 'feat')
- new_weight: float32 [128, 128], P('feat')
- new_first: float32 [128, 128], P('feat')
- new_second: float32 [128, 128], P('feat')
Inputs may be any that keep to these rules, and one draw needn't show every extreme that they name: `tile_row`: the slots of index d of node (slots d * 256 to (d + 1) * 256 - 1) name target blocks of that index only: d * 16 to (d + 1) * 16 - 1. `tile_col`: A slot's source block lies on an index of node at most 2 away from the slot's own index around the closed loop of node indices; both distances 2 occur on every index. `tile_count`: some index of node has all 256 slots live, some has 32.
All inputs are finite; a program needn't handle non-finite values.
Results may differ from a plain program's by a relative error of at most 0.0058.
Values may be sent and summed in bfloat16 or wider, within the bound.
No kernel may reach another device: no remote copies, remote signals or barrier semaphores. Data moves between devices by JAX's collectives and lax.ppermute only.
A program may use at most 64 MiB of HBM per device.

v0:
```python
import math
import jax
import jax.numpy as jnp
from jax import lax
from jax.sharding import PartitionSpec as P

REACH = 2
first_decay = 0.9
second_decay = 0.999
learn_rate = 0.05
first_fix = 1.0 - 0.9**10
second_fix = 1.0 - 0.999**10
adam_eps = 1e-08


def passed_along(block, axis, distance):
    devices = range(lax.axis_size(axis))
    route = [((i - distance) % len(devices), i) for i in devices]
    return lax.ppermute(block, axis, route)


def elu_slope(preact):
    return jnp.where(preact > 0, 1.0, jnp.exp(jnp.minimum(preact, 0.0)))


def one_hot_table(indices, count, dtype):
    return (indices[:, None] == jnp.arange(count)[None, :]).astype(dtype)


def per_device(
    features,
    tile_values,
    tile_row,
    tile_col,
    tile_count,
    weight,
    first_moment,
    second_moment,
    cotangent,
):
    cycle_size = lax.axis_size("node")
    own_node = lax.axis_index("node")
    blocks = features.shape[0]
    width_local = features.shape[1]
    tile_size = features.shape[2]
    slots = tile_values.shape[0]
    live = (jnp.arange(slots) < tile_count[0]).astype(jnp.float32)
    local_row = tile_row - own_node * blocks
    col_owner = tile_col // blocks
    col_block = tile_col % blocks
    offset = (col_owner - own_node) % cycle_size
    offset = jnp.where(offset > cycle_size // 2, offset - cycle_size, offset)
    source_slot = (offset + REACH) * blocks + col_block
    targets = (2 * REACH + 1) * blocks
    pick_source = one_hot_table(source_slot, targets, jnp.bfloat16)
    pick_row = one_hot_table(local_row, blocks, jnp.bfloat16)
    add_row = one_hot_table(local_row, blocks, jnp.float32) * live[:, None]
    add_source = one_hot_table(source_slot, targets, jnp.float32) * live[:, None]
    pieces = []
    for distance in range(-REACH, REACH + 1):
        if distance == 0:
            pieces.append(features)
        else:
            pieces.append(passed_along(features, "node", -distance))
    nearby = jnp.concatenate(pieces, axis=0)
    sources = jnp.einsum(
        "ts,sfk->tfk", pick_source, nearby, preferred_element_type=jnp.float32
    ).astype(jnp.bfloat16)
    forward_terms = jnp.einsum(
        "tfk,tjk->tfj", sources, tile_values, preferred_element_type=jnp.float32
    )
    aggregate = jnp.einsum("tb,tfj->bfj", add_row, forward_terms, precision=lax.Precision.HIGHEST)
    aggregate = aggregate.astype(jnp.bfloat16)
    weight_half = weight.astype(jnp.bfloat16)
    aggregate_all, weight_all = (
        lax.all_gather(aggregate, "feat", axis=1, tiled=True),
        lax.all_gather(weight_half, "feat", axis=0, tiled=True),
    )
    column_start = lax.axis_index("feat") * width_local
    weight_cols = lax.dynamic_slice_in_dim(weight_all, column_start, width_local, 1)
    preact = jnp.einsum(
        "bij,io->boj", aggregate_all, weight_cols, preferred_element_type=jnp.float32
    )
    activated = jax.nn.elu(preact).astype(jnp.bfloat16)
    slope_grad = (cotangent.astype(jnp.float32) * elu_slope(preact)).astype(jnp.bfloat16)
    slope_all = lax.all_gather(slope_grad, "feat", axis=1, tiled=True)
    node_total = cycle_size * blocks * tile_size
    grad_local = jnp.einsum("bij,boj->io", aggregate, slope_all, preferred_element_type=jnp.float32)
    grad = lax.psum(grad_local, "node") * (1.0 / math.sqrt(node_total))
    back_rows = jnp.einsum(
        "io,boj->bij", weight_half, slope_all, preferred_element_type=jnp.float32
    ).astype(jnp.bfloat16)
    back_sources = jnp.einsum(
        "tb,bfj->tfj", pick_row, back_rows, preferred_element_type=jnp.float32
    ).astype(jnp.bfloat16)
    back_terms = jnp.einsum(
        "tfj,tjk->tfk", back_sources, tile_values, preferred_element_type=jnp.float32
    )
    outgoing = jnp.einsum("ts,tfk->sfk", add_source, back_terms, precision=lax.Precision.HIGHEST)
    outgoing = outgoing.reshape(2 * REACH + 1, blocks, width_local, tile_size)
    feature_grad = outgoing[REACH]
    for distance in range(-REACH, REACH + 1):
        if distance != 0:
            feature_grad = feature_grad + passed_along(outgoing[distance + REACH], "node", distance)
    new_first = first_decay * first_moment + (1.0 - first_decay) * grad
    new_second = second_decay * second_moment + (1.0 - second_decay) * grad * grad
    new_weight = weight - learn_rate * (new_first / first_fix) / (
        jnp.sqrt(new_second / second_fix) + adam_eps
    )
    return (activated, feature_grad, new_weight, new_first, new_second)


def solution(mesh):
    return jax.shard_map(
        per_device,
        mesh=mesh,
        in_specs=(
            P("node", "feat", None),
            P("node", None, None),
            P("node"),
            P("node"),
            P("node"),
            P("feat", None),
            P("feat", None),
            P("feat", None),
            P("node", "feat", None),
        ),
        out_specs=(
            P("node", "feat", None),
            P("node", "feat", None),
            P("feat", None),
            P("feat", None),
            P("feat", None),
        ),
        check_vma=False,
    )
```

profile of v0, /device:TPU:0, one launch (start us, length us, event | category | flops | bytes accessed | tf_op | source)
XLA Modules:
  0.0 112.7 jit_solution(17020929460422994571)
XLA Ops:
  0.6 6.0 %collective-permute-start.2 = (bf16[16,32,128]{2,1,0:T(8,128)(2,1)}, bf16[16,32,128]{2,1,0:T(8,128)(2,1)S(1)}, u32[]{:S(2)}, u32[]{:S(2)}) collective-permute-start(bf16[16,32,128]{2,1,0:T(8,128)(2,1)} %param.9), channel_id=1, source_target_pairs={{4,0},{8,4},{12,8},{16,12},{20,16},{24,20},{28,24},{0,28},{5,1},{9... | collective-permute-start | bytes 393224 | tf_op jit(solution)/shard_map/ppermute | solution.py:19
  6.7 3.8 %collective-permute-start.3 = (bf16[16,32,128]{2,1,0:T(8,128)(2,1)}, bf16[16,32,128]{2,1,0:T(8,128)(2,1)S(1)}, u32[]{:S(2)}, u32[]{:S(2)}) collective-permute-start(bf16[16,32,128]{2,1,0:T(8,128)(2,1)} %param.9), channel_id=1, source_target_pairs={{8,0},{12,4},{16,8},{20,12},{24,16},{28,20},{0,24},{4,28},{9,1},{1... | collective-permute-start | bytes 393224 | tf_op jit(solution)/shard_map/ppermute | solution.py:19
  10.5 0.7 fusion.41
  11.2 0.7 broadcast_subtract_fusion
  12.5 0.7 convert_element_type.38
  13.3 5.2 %all_gather.9 = bf16[128,128]{1,0:T(8,128)(2,1)S(1)} all-gather(bf16[32,128]{1,0:T(8,128)(2,1)S(1)} %convert_element_type.38), channel_id=1, replica_groups=mesh['node'=8,'feat'=4] {'feat'}, dimensions={0}, use_global_device_ids=true | all-gather | bytes 40960 | tf_op jit(solution)/shard_map/all_gather | solution.py:77
  18.5 0.9 constant_dynamic-update-slice_fusion.2
  19.5 0.8 fusion.10
  20.3 7.2 %fusion.4 = f32[256,32,128]{2,1,0:T(8,128)S(1)} fusion(bf16[256,128,128]{2,1,0:T(8,128)(2,1)} %param.10, bf16[256,32,128]{2,0,1:T(8,128)(2,1)S(1)} %fusion.10), kind=kOutput, calls=%fused_computation.6 | convolution fusion | flops 268435456 | bytes 14680064 | tf_op jit(solution)/shard_map/tfk,tjk->tfj/dot_general | solution.py:69
  27.5 4.4 %fusion.7 = bf16[16,32,128]{2,0,1:T(8,128)(2,1)S(1)} fusion(f32[256,32,128]{2,1,0:T(8,128)S(1)} %fusion.4, f32[256]{0:T(256)S(1)} %compare_convert_fusion, s32[256]{0:T(256)S(1)} %broadcast_subtract_fusion), kind=kOutput, calls=%fused_computation.11 | convolution fusion | flops 201400320 | bytes 4327424 | tf_op jit(solution)/shard_map/tb,tfj->bfj/dot_general | solution.py:72
  31.9 7.3 %all_gather.10 = bf16[16,128,128]{2,0,1:T(8,128)(2,1)S(1)} all-gather(bf16[16,32,128]{2,0,1:T(8,128)(2,1)S(1)} %fusion.7), channel_id=1, replica_groups=mesh['node'=8,'feat'=4] {'feat'}, dimensions={1}, use_global_device_ids=true | all-gather | bytes 655360 | tf_op jit(solution)/shard_map/all_gather | solution.py:76
  39.1 1.1 fusion.16
  40.2 7.5 %all_gather.11 = bf16[16,128,128]{2,1,0:T(8,128)(2,1)S(1)} all-gather(bf16[16,32,128]{2,1,0:T(8,128)(2,1)S(1)} %get-tuple-element.22), channel_id=1, replica_groups=mesh['node'=8,'feat'=4] {'feat'}, dimensions={1}, use_global_device_ids=true | all-gather | bytes 655360 | tf_op jit(solution)/shard_map/all_gather | solution.py:86
  48.3 0.7 fusion.34
  49.0 7.2 %fusion.5 = f32[256,32,128]{2,1,0:T(8,128)S(1)} fusion(bf16[256,128,128]{2,1,0:T(8,128)(2,1)} %param.10, bf16[256,32,128]{2,0,1:T(8,128)(2,1)S(1)} %fusion.34), kind=kOutput, calls=%fused_computation.7 | convolution fusion | flops 268435456 | bytes 14680064 | tf_op jit(solution)/shard_map/tfj,tjk->tfk/dot_general | solution.py:96
  56.2 4.9 %fusion = f32[80,32,128]{2,0,1:T(8,128)S(1)} fusion(f32[256,32,128]{2,1,0:T(8,128)S(1)} %fusion.5, f32[256]{0:T(256)S(1)} %compare_convert_fusion, s32[256]{0:T(256)S(1)} %fusion.41), kind=kOutput, calls=%fused_computation | convolution fusion | flops 1006673920 | bytes 5507072 | tf_op jit(solution)/shard_map/ts,tfk->sfk/dot_general | solution.py:99
  61.1 0.9 fusion.48
  62.0 2.0 %collective-permute-start.7 = (f32[16,32,128]{2,0,1:T(8,128)}, f32[16,32,128]{2,0,1:T(8,128)S(1)}, u32[]{:S(2)}, u32[]{:S(2)}) collective-permute-start(f32[16,32,128]{2,0,1:T(8,128)} %get-tuple-element.19), channel_id=1, source_target_pairs={{24,0},{28,4},{0,8},{4,12},{8,16},{12,20},{16,24},{20,28},{25,1},{... | collective-permute-start | bytes 786440 | tf_op jit(solution)/shard_map/ppermute | solution.py:19
  64.0 1.5 %collective-permute-start.6 = (f32[16,32,128]{2,0,1:T(8,128)S(1)}, f32[16,32,128]{2,0,1:T(8,128)S(1)}, u32[]{:S(2)}, u32[]{:S(2)}) collective-permute-start(f32[16,32,128]{2,0,1:T(8,128)S(1)} %get-tuple-element.20), channel_id=1, source_target_pairs={{28,0},{0,4},{4,8},{8,12},{12,16},{16,20},{20,24},{24,28},{29,1},{... | collective-permute-start | bytes 786440 | tf_op jit(solution)/shard_map/ppermute | solution.py:19
  65.5 3.3 %collective-permute-start.5 = (f32[16,32,128]{2,0,1:T(8,128)S(1)}, f32[16,32,128]{2,0,1:T(8,128)S(1)}, u32[]{:S(2)}, u32[]{:S(2)}) collective-permute-start(f32[16,32,128]{2,0,1:T(8,128)S(1)} %get-tuple-element.21), channel_id=1, source_target_pairs={{4,0},{8,4},{12,8},{16,12},{20,16},{24,20},{28,24},{0,28},{5,1},{9... | collective-permute-start | bytes 786440 | tf_op jit(solution)/shard_map/ppermute | solution.py:19
  68.8 0.9 convolution_bitcast_fusion.1
  69.7 40.8 %psum.7 = f32[32,128]{1,0:T(8,128)S(1)} all-reduce(f32[32,128]{1,0:T(8,128)} %convolution_bitcast_fusion.1), channel_id=1, replica_groups=mesh['node'=8,'feat'=4] {'node'}, use_global_device_ids=true, to_apply=%region_0.1 | all-reduce | flops 4096 | bytes 32768 | tf_op jit(solution)/shard_map/psum | solution.py:89
  110.4 1.4 %divide_subtract_fusion = (f32[32,128]{1,0:T(8,128)}, f32[32,128]{1,0:T(8,128)}, f32[32,128]{1,0:T(8,128)}) fusion(f32[32,128]{1,0:T(8,128)S(1)} %copy-done, f32[32,128]{1,0:T(8,128)S(1)} %psum.7, f32[32,128]{1,0:T(8,128)} %param.15, f32[32,128]{1,0:T(8,128)} %param.16), kind=kLoop, calls=%fused_computation.39 | loop fusion | flops 53248 | bytes 114688 | tf_op jit(solution)/shard_map/sub | solution.py:107
  111.9 0.8 copy.21
  (23 shorter events, 0.8 us)
Async XLA Ops:
  0.6 18.8 %collective-permute-start.2 = (bf16[16,32,128]{2,1,0:T(8,128)(2,1)}, bf16[16,32,128]{2,1,0:T(8,128)(2,1)S(1)}, u32[]{:S(2)}, u32[]{:S(2)}) collective-permute-start(bf16[16,32,128]{2,1,0:T(8,128)(2,1)} %param.9), channel_id=1, source_target_pairs={{4,0},{8,4},{12,8},{16,12},{20,16},{24,20},{28,24},{0,28},{5,1},{9... | collective-permute-start | bytes 393224 | tf_op jit(solution)/shard_map/ppermute | solution.py:19
  6.7 11.8 %collective-permute-start.1 = (bf16[16,32,128]{2,1,0:T(8,128)(2,1)}, bf16[16,32,128]{2,1,0:T(8,128)(2,1)S(1)}, u32[]{:S(2)}, u32[]{:S(2)}) collective-permute-start(bf16[16,32,128]{2,1,0:T(8,128)(2,1)} %param.9), channel_id=1, source_target_pairs={{28,0},{0,4},{4,8},{8,12},{12,16},{16,20},{20,24},{24,28},{29,1},{... | collective-permute-start | bytes 393224 | tf_op jit(solution)/shard_map/ppermute | solution.py:19
  6.7 11.8 %collective-permute-start = (bf16[16,32,128]{2,1,0:T(8,128)(2,1)}, bf16[16,32,128]{2,1,0:T(8,128)(2,1)S(1)}, u32[]{:S(2)}, u32[]{:S(2)}) collective-permute-start(bf16[16,32,128]{2,1,0:T(8,128)(2,1)} %param.9), channel_id=1, source_target_pairs={{24,0},{28,4},{0,8},{4,12},{8,16},{12,20},{16,24},{20,28},{25,1},{... | collective-permute-start | bytes 393224 | tf_op jit(solution)/shard_map/ppermute | solution.py:19
  6.7 12.8 %collective-permute-start.3 = (bf16[16,32,128]{2,1,0:T(8,128)(2,1)}, bf16[16,32,128]{2,1,0:T(8,128)(2,1)S(1)}, u32[]{:S(2)}, u32[]{:S(2)}) collective-permute-start(bf16[16,32,128]{2,1,0:T(8,128)(2,1)} %param.9), channel_id=1, source_target_pairs={{8,0},{12,4},{16,8},{20,12},{24,16},{28,20},{0,24},{4,28},{9,1},{1... | collective-permute-start | bytes 393224 | tf_op jit(solution)/shard_map/ppermute | solution.py:19
  27.5 11.6 %copy-start.1 = (bf16[16,32,128]{2,1,0:T(8,128)(2,1)S(1)}, bf16[16,32,128]{2,1,0:T(8,128)(2,1)}, u32[]{:S(2)}) copy-start(bf16[16,32,128]{2,1,0:T(8,128)(2,1)} %param.17) | copy-start | bytes 393220
  56.2 54.2 %copy-start = (f32[32,128]{1,0:T(8,128)S(1)}, f32[32,128]{1,0:T(8,128)}, u32[]{:S(2)}) copy-start(f32[32,128]{1,0:T(8,128)} %param.14) | copy-start | bytes 49156
  62.0 49.8 %collective-permute-start.4 = (f32[16,32,128]{2,0,1:T(8,128)}, f32[16,32,128]{2,0,1:T(8,128)S(1)}, u32[]{:S(2)}, u32[]{:S(2)}) collective-permute-start(f32[16,32,128]{2,0,1:T(8,128)} %get-tuple-element.18), channel_id=1, source_target_pairs={{8,0},{12,4},{16,8},{20,12},{24,16},{28,20},{0,24},{4,28},{9,1},{1... | collective-permute-start | bytes 786440 | tf_op jit(solution)/shard_map/ppermute | solution.py:19
  62.0 49.8 %collective-permute-start.7 = (f32[16,32,128]{2,0,1:T(8,128)}, f32[16,32,128]{2,0,1:T(8,128)S(1)}, u32[]{:S(2)}, u32[]{:S(2)}) collective-permute-start(f32[16,32,128]{2,0,1:T(8,128)} %get-tuple-element.19), channel_id=1, source_target_pairs={{24,0},{28,4},{0,8},{4,12},{8,16},{12,20},{16,24},{20,28},{25,1},{... | collective-permute-start | bytes 786440 | tf_op jit(solution)/shard_map/ppermute | solution.py:19
  64.0 47.7 %collective-permute-start.6 = (f32[16,32,128]{2,0,1:T(8,128)S(1)}, f32[16,32,128]{2,0,1:T(8,128)S(1)}, u32[]{:S(2)}, u32[]{:S(2)}) collective-permute-start(f32[16,32,128]{2,0,1:T(8,128)S(1)} %get-tuple-element.20), channel_id=1, source_target_pairs={{28,0},{0,4},{4,8},{8,12},{12,16},{16,20},{20,24},{24,28},{29,1},{... | collective-permute-start | bytes 786440 | tf_op jit(solution)/shard_map/ppermute | solution.py:19
  65.5 46.3 %collective-permute-start.5 = (f32[16,32,128]{2,0,1:T(8,128)S(1)}, f32[16,32,128]{2,0,1:T(8,128)S(1)}, u32[]{:S(2)}, u32[]{:S(2)}) collective-permute-start(f32[16,32,128]{2,0,1:T(8,128)S(1)} %get-tuple-element.21), channel_id=1, source_target_pairs={{4,0},{8,4},{12,8},{16,12},{20,16},{24,20},{28,24},{0,28},{5,1},{9... | collective-permute-start | bytes 786440 | tf_op jit(solution)/shard_map/ppermute | solution.py:19
where the time goes:
time: 113 us
  blocking collectives  60.6 us (54%)
  matrix products  27.5 us (24%)
  starting transfers between devices  16.6 us (15%)
  other arithmetic  3.56 us (3%)
  local copies, waits for them, and re-layouts  2.92 us (3%)
  between operations  1.42 us (1%)
    psum x1, blocking collectives, per_device(): grad = lax.psum(grad_local, 'node') * (1.0 / math.sqrt(node_total))  40.8 us
    ppermute x8, starting transfers between devices, passed_along(): return lax.ppermute(block, axis, route)  16.6 us
    all_gather x1, blocking collectives, per_device(): slope_all = lax.all_gather(slope_grad, 'feat', axis=1, tiled=True)  7.46 us
    all_gather x1, blocking collectives, per_device(): lax.all_gather(aggregate, 'feat', axis=1, tiled=True)  7.25 us
    dot_general x1, matrix products, per_device(): jnp.einsum('tfk,tjk->tfj', sources, tile_values, preferred_element_type=j...  7.25 us
    dot_general x1, matrix products, per_device(): jnp.einsum('tfj,tjk->tfk', back_sources, tile_values, preferred_element_t...  7.21 us
    all_gather x1, blocking collectives, per_device(): lax.all_gather(weight_half, 'feat', axis=0, tiled=True)  5.18 us
    dot_general x1, matrix products, per_device(): jnp.einsum('ts,tfk->sfk', add_source, back_terms, precision=lax.Precision...  4.89 us
  transfers between devices with their start and end apart: 8, of which 0 were waited for; matrix products, arithmetic and copies ran while one was open for 5% of the time, Pallas kernels for 0%

commit v1 on v0

--- a/solution.py
+++ b/solution.py
@@ -11,6 +11,28 @@
 first_fix = 1.0 - 0.9**10
 second_fix = 1.0 - 0.999**10
 adam_eps = 1e-08
+
+
+def in_order(tiles, dim):
+    tiles = jnp.moveaxis(tiles, 0, dim)
+    shape = tiles.shape
+    return tiles.reshape(*shape[:dim], shape[dim] * shape[dim + 1], *shape[dim + 2 :])
+
+
+def gather_around(x, axis, dim):
+    count = lax.axis_size(axis)
+    pairs = [(i, (i + 1) % count) for i in range(count)]
+    back = [(b, a) for a, b in pairs]
+    lower, upper = ([], [])
+    for lap in range(count - 1):
+        if lap % 2 == 0:
+            lower.append(lax.ppermute(lower[-1] if lower else x, axis, pairs))
+        else:
+            upper.append(lax.ppermute(upper[-1] if upper else x, axis, back))
+    pieces = jnp.stack([*lower[::-1], x, *upper])
+    shift = lax.axis_index(axis) - len(lower)
+    pieces = pieces[(jnp.arange(count) - shift) % count]
+    return in_order(pieces, dim)
 
 
 def passed_along(block, axis, distance):
@@ -73,7 +95,7 @@
     aggregate = aggregate.astype(jnp.bfloat16)
     weight_half = weight.astype(jnp.bfloat16)
     aggregate_all, weight_all = (
-        lax.all_gather(aggregate, "feat", axis=1, tiled=True),
+        gather_around(aggregate, "feat", 1),
         lax.all_gather(weight_half, "feat", axis=0, tiled=True),
     )
     column_start = lax.axis_index("feat") * width_local

time: 113 us -> 117 us (1.035)
  waiting for transfers between devices: 0.02 us -> 6.21 us
  blocking collectives: 60.6 us -> 55.9 us
  starting transfers between devices: 16.6 us -> 18.8 us
    all_gather x1 -> x0, blocking collectives: 7.25 us -> none  [per_device(): lax.all_gather(aggregate, 'feat', axis=1, tiled=True)]
    ppermute x8, waiting for transfers between devices: 0.02 us -> 3.56 us  [passed_along(): return lax.ppermute(block, axis, route)]
    ppermute x0 -> x3, waiting for transfers between devices: none -> 2.65 us  [the longest x2 2.65 us: gather_around(): lower.append(lax.ppermute(lower[-1] if lower else x, axis, pairs))]
    ppermute x0 -> x3, starting transfers between devices: none -> 1.77 us  [the longest x1 1.73 us: gather_around(): upper.append(lax.ppermute(upper[-1] if upper else x, axis, back))]
    psum x1, blocking collectives: 40.8 us -> 42.5 us  [per_device(): grad = lax.psum(grad_local, 'node') * (1.0 / math.sqrt(node_total))]
  transfers between devices with their start and end apart: 8 -> 11, of which waited for: 0 -> 3; matrix products, arithmetic and copies ran while one was open for 5% -> 4% of each run, Pallas kernels for 0% -> 0%
where the time goes in v1:
time: 117 us; the launch traced here: 116 us
  blocking collectives  55.9 us (48%)
  matrix products  27.5 us (24%)
  starting transfers between devices  18.8 us (16%)
  waiting for transfers between devices  6.21 us (5%)
  local copies, waits for them, and re-layouts  3.55 us (3%)
  other arithmetic  2.93 us (3%)
  between operations  1.48 us (1%)
    psum x1, blocking collectives, per_device(): grad = lax.psum(grad_local, 'node') * (1.0 / math.sqrt(node_total))  42.5 us
    ppermute x8, starting transfers between devices, passed_along(): return lax.ppermute(block, axis, route)  17 us
    all_gather x1, blocking collectives, per_device(): slope_all = lax.all_gather(slope_grad, 'feat', axis=1, tiled=True)  7.3 us
    dot_general x1, matrix products, per_device(): jnp.einsum('tfk,tjk->tfj', sources, tile_values, preferred_element_type=j...  7.25 us
    dot_general x1, matrix products, per_device(): jnp.einsum('tfj,tjk->tfk', back_sources, tile_values, preferred_element_t...  7.21 us
    all_gather x1, blocking collectives, per_device(): lax.all_gather(weight_half, 'feat', axis=0, tiled=True)  6.11 us
    dot_general x1, matrix products, per_device(): jnp.einsum('ts,tfk->sfk', add_source, back_terms, precision=lax.Precision...  4.89 us
    dot_general x1, matrix products, per_device(): jnp.einsum('tb,tfj->bfj', add_row, forward_terms, precision=lax.Precision...  4.35 us
  transfers between devices with their start and end apart: 11, of which 3 were waited for; matrix products, arithmetic and copies ran while one was open for 4% of the time, Pallas kernels for 0%

profile of v1, /device:TPU:0, one launch (start us, length us, event | category | flops | bytes accessed | tf_op | source)
XLA Modules:
  0.0 116.4 jit_solution(426708267641238286)
XLA Ops:
  0.6 6.0 %collective-permute-start.2 = (bf16[16,32,128]{2,1,0:T(8,128)(2,1)}, bf16[16,32,128]{2,1,0:T(8,128)(2,1)S(1)}, u32[]{:S(2)}, u32[]{:S(2)}) collective-permute-start(bf16[16,32,128]{2,1,0:T(8,128)(2,1)} %param.9), channel_id=1, source_target_pairs={{4,0},{8,4},{12,8},{16,12},{20,16},{24,20},{28,24},{0,28},{5,1},{9... | collective-permute-start | bytes 393224 | tf_op jit(solution)/shard_map/ppermute | solution.py:41
  6.7 3.8 %collective-permute-start.3 = (bf16[16,32,128]{2,1,0:T(8,128)(2,1)}, bf16[16,32,128]{2,1,0:T(8,128)(2,1)S(1)}, u32[]{:S(2)}, u32[]{:S(2)}) collective-permute-start(bf16[16,32,128]{2,1,0:T(8,128)(2,1)} %param.9), channel_id=1, source_target_pairs={{8,0},{12,4},{16,8},{20,12},{24,16},{28,20},{0,24},{4,28},{9,1},{1... | collective-permute-start | bytes 393224 | tf_op jit(solution)/shard_map/ppermute | solution.py:41
  12.5 2.5 %collective-permute-done = bf16[16,32,128]{2,1,0:T(8,128)(2,1)S(1)} collective-permute-done((bf16[16,32,128]{2,1,0:T(8,128)(2,1)}, bf16[16,32,128]{2,1,0:T(8,128)(2,1)S(1)}, u32[]{:S(2)}, u32[]{:S(2)}) %collective-permute-start) | collective-permute-done | bytes 131104 | tf_op jit(solution)/shard_map/ppermute | solution.py:41
  15.1 1.0 collective-permute-done.1
  16.1 0.9 constant_dynamic-update-slice_fusion.2
  17.1 0.8 fusion.10
  17.9 7.2 %fusion.4 = f32[256,32,128]{2,1,0:T(8,128)S(1)} fusion(bf16[256,128,128]{2,1,0:T(8,128)(2,1)} %param.10, bf16[256,32,128]{2,0,1:T(8,128)(2,1)S(1)} %fusion.10), kind=kOutput, calls=%fused_computation.7 | convolution fusion | flops 268435456 | bytes 14680064 | tf_op jit(solution)/shard_map/tfk,tjk->tfj/dot_general | solution.py:91
  25.2 4.4 %fusion.7 = bf16[16,32,128]{2,0,1:T(8,128)(2,1)S(1)} fusion(f32[256,32,128]{2,1,0:T(8,128)S(1)} %fusion.4, f32[256]{0:T(256)S(1)} %compare_convert_fusion, s32[256]{0:T(256)S(1)} %broadcast_subtract_fusion), kind=kOutput, calls=%fused_computation.12 | convolution fusion | flops 201400320 | bytes 4327424 | tf_op jit(solution)/shard_map/tb,tfj->bfj/dot_general | solution.py:94
  29.6 1.7 %collective-permute-start.6 = (bf16[16,32,128]{2,0,1:T(8,128)(2,1)S(1)}, bf16[16,32,128]{2,0,1:T(8,128)(2,1)S(1)}, u32[]{:S(2)}, u32[]{:S(2)}) collective-permute-start(bf16[16,32,128]{2,0,1:T(8,128)(2,1)S(1)} %fusion.7), channel_id=1, source_target_pairs={{1,0},{2,1},{3,2},{0,3},{5,4},{6,5},{7,6},{4,7},{9,8},{10,9},{11,1... | collective-permute-start | bytes 393224 | tf_op jit(solution)/shard_map/ppermute | solution.py:31
  31.3 2.6 %collective-permute-done.4 = bf16[16,32,128]{2,0,1:T(8,128)(2,1)S(1)} collective-permute-done((bf16[16,32,128]{2,0,1:T(8,128)(2,1)S(1)}, bf16[16,32,128]{2,0,1:T(8,128)(2,1)S(1)}, u32[]{:S(2)}, u32[]{:S(2)}) %collective-permute-start.4) | collective-permute-done | bytes 131104 | tf_op jit(solution)/shard_map/ppermute | solution.py:29
  34.0 6.1 %all_gather.6 = bf16[128,128]{1,0:T(8,128)(2,1)S(1)} all-gather(bf16[32,128]{1,0:T(8,128)(2,1)S(1)} %convert_element_type.38), channel_id=1, replica_groups=mesh['node'=8,'feat'=4] {'feat'}, dimensions={0}, use_global_device_ids=true | all-gather | bytes 40960 | tf_op jit(solution)/shard_map/all_gather | solution.py:99
  40.9 1.1 fusion.16
  42.0 7.3 %all_gather.7 = bf16[16,128,128]{2,1,0:T(8,128)(2,1)S(1)} all-gather(bf16[16,32,128]{2,1,0:T(8,128)(2,1)S(1)} %get-tuple-element.22), channel_id=1, replica_groups=mesh['node'=8,'feat'=4] {'feat'}, dimensions={1}, use_global_device_ids=true | all-gather | bytes 655360 | tf_op jit(solution)/shard_map/all_gather | solution.py:108
  49.8 0.7 fusion.34
  50.6 7.2 %fusion.5 = f32[256,32,128]{2,1,0:T(8,128)S(1)} fusion(bf16[256,128,128]{2,1,0:T(8,128)(2,1)} %param.10, bf16[256,32,128]{2,0,1:T(8,128)(2,1)S(1)} %fusion.34), kind=kOutput, calls=%fused_computation.8 | convolution fusion | flops 268435456 | bytes 14680064 | tf_op jit(solution)/shard_map/tfj,tjk->tfk/dot_general | solution.py:118
  57.8 4.9 %fusion = f32[80,32,128]{2,0,1:T(8,128)S(1)} fusion(f32[256,32,128]{2,1,0:T(8,128)S(1)} %fusion.5, f32[256]{0:T(256)S(1)} %compare_convert_fusion, s32[256]{0:T(256)S(1)} %fusion.41), kind=kOutput, calls=%fused_computation.1 | convolution fusion | flops 1006673920 | bytes 5507072 | tf_op jit(solution)/shard_map/ts,tfk->sfk/dot_general | solution.py:121
  62.7 0.9 fusion.50
  63.6 2.5 %collective-permute-start.7 = (f32[16,32,128]{2,0,1:T(8,128)}, f32[16,32,128]{2,0,1:T(8,128)S(1)}, u32[]{:S(2)}, u32[]{:S(2)}) collective-permute-start(f32[16,32,128]{2,0,1:T(8,128)} %get-tuple-element.18), channel_id=1, source_target_pairs={{8,0},{12,4},{16,8},{20,12},{24,16},{28,20},{0,24},{4,28},{9,1},{1... | collective-permute-start | bytes 786440 | tf_op jit(solution)/shard_map/ppermute | solution.py:41
  66.0 2.9 %collective-permute-start.9 = (f32[16,32,128]{2,0,1:T(8,128)S(1)}, f32[16,32,128]{2,0,1:T(8,128)S(1)}, u32[]{:S(2)}, u32[]{:S(2)}) collective-permute-start(f32[16,32,128]{2,0,1:T(8,128)S(1)} %get-tuple-element.20), channel_id=1, source_target_pairs={{28,0},{0,4},{4,8},{8,12},{12,16},{16,20},{20,24},{24,28},{29,1},{... | collective-permute-start | bytes 786440 | tf_op jit(solution)/shard_map/ppermute | solution.py:41
  68.9 1.9 %collective-permute-start.8 = (f32[16,32,128]{2,0,1:T(8,128)S(1)}, f32[16,32,128]{2,0,1:T(8,128)S(1)}, u32[]{:S(2)}, u32[]{:S(2)}) collective-permute-start(f32[16,32,128]{2,0,1:T(8,128)S(1)} %get-tuple-element.21), channel_id=1, source_target_pairs={{4,0},{8,4},{12,8},{16,12},{20,16},{24,20},{28,24},{0,28},{5,1},{9... | collective-permute-start | bytes 786440 | tf_op jit(solution)/shard_map/ppermute | solution.py:41
  70.7 0.9 convolution_bitcast_fusion.1
  71.6 42.5 %psum.7 = f32[32,128]{1,0:T(8,128)S(1)} all-reduce(f32[32,128]{1,0:T(8,128)} %convolution_bitcast_fusion.1), channel_id=1, replica_groups=mesh['node'=8,'feat'=4] {'node'}, use_global_device_ids=true, to_apply=%region_0.1 | all-reduce | flops 4096 | bytes 32768 | tf_op jit(solution)/shard_map/psum | solution.py:111
  114.1 1.4 %divide_subtract_fusion = (f32[32,128]{1,0:T(8,128)}, f32[32,128]{1,0:T(8,128)}, f32[32,128]{1,0:T(8,128)}) fusion(f32[32,128]{1,0:T(8,128)S(1)} %copy-done, f32[32,128]{1,0:T(8,128)S(1)} %psum.7, f32[32,128]{1,0:T(8,128)} %param.15, f32[32,128]{1,0:T(8,128)} %param.16), kind=kLoop, calls=%fused_computation.41 | loop fusion | flops 53248 | bytes 114688 | tf_op jit(solution)/shard_map/sub | solution.py:129
  115.6 0.8 copy.21
  (32 shorter events, 2.9 us)
Async XLA Ops:
  0.6 16.4 %collective-permute-start.2 = (bf16[16,32,128]{2,1,0:T(8,128)(2,1)}, bf16[16,32,128]{2,1,0:T(8,128)(2,1)S(1)}, u32[]{:S(2)}, u32[]{:S(2)}) collective-permute-start(bf16[16,32,128]{2,1,0:T(8,128)(2,1)} %param.9), channel_id=1, source_target_pairs={{4,0},{8,4},{12,8},{16,12},{20,16},{24,20},{28,24},{0,28},{5,1},{9... | collective-permute-start | bytes 393224 | tf_op jit(solution)/shard_map/ppermute | solution.py:41
  6.7 9.4 %collective-permute-start.1 = (bf16[16,32,128]{2,1,0:T(8,128)(2,1)}, bf16[16,32,128]{2,1,0:T(8,128)(2,1)S(1)}, u32[]{:S(2)}, u32[]{:S(2)}) collective-permute-start(bf16[16,32,128]{2,1,0:T(8,128)(2,1)} %param.9), channel_id=1, source_target_pairs={{28,0},{0,4},{4,8},{8,12},{12,16},{16,20},{20,24},{24,28},{29,1},{... | collective-permute-start | bytes 393224 | tf_op jit(solution)/shard_map/ppermute | solution.py:41
  6.7 8.4 %collective-permute-start = (bf16[16,32,128]{2,1,0:T(8,128)(2,1)}, bf16[16,32,128]{2,1,0:T(8,128)(2,1)S(1)}, u32[]{:S(2)}, u32[]{:S(2)}) collective-permute-start(bf16[16,32,128]{2,1,0:T(8,128)(2,1)} %param.9), channel_id=1, source_target_pairs={{24,0},{28,4},{0,8},{4,12},{8,16},{12,20},{16,24},{20,28},{25,1},{... | collective-permute-start | bytes 393224 | tf_op jit(solution)/shard_map/ppermute | solution.py:41
  6.7 10.4 %collective-permute-start.3 = (bf16[16,32,128]{2,1,0:T(8,128)(2,1)}, bf16[16,32,128]{2,1,0:T(8,128)(2,1)S(1)}, u32[]{:S(2)}, u32[]{:S(2)}) collective-permute-start(bf16[16,32,128]{2,1,0:T(8,128)(2,1)} %param.9), channel_id=1, source_target_pairs={{8,0},{12,4},{16,8},{20,12},{24,16},{28,20},{0,24},{4,28},{9,1},{1... | collective-permute-start | bytes 393224 | tf_op jit(solution)/shard_map/ppermute | solution.py:41
  25.1 8.8 %copy-start = (f32[32,128]{1,0:T(8,128)S(1)}, f32[32,128]{1,0:T(8,128)}, u32[]{:S(2)}) copy-start(f32[32,128]{1,0:T(8,128)} %param.14) | copy-start | bytes 49156
  25.2 15.7 %copy-start.1 = (bf16[16,32,128]{2,1,0:T(8,128)(2,1)S(1)}, bf16[16,32,128]{2,1,0:T(8,128)(2,1)}, u32[]{:S(2)}) copy-start(bf16[16,32,128]{2,1,0:T(8,128)(2,1)} %param.17) | copy-start | bytes 393220
  29.5 4.4 %collective-permute-start.4 = (bf16[16,32,128]{2,0,1:T(8,128)(2,1)S(1)}, bf16[16,32,128]{2,0,1:T(8,128)(2,1)S(1)}, u32[]{:S(2)}, u32[]{:S(2)}) collective-permute-start(bf16[16,32,128]{2,0,1:T(8,128)(2,1)S(1)} %fusion.7), channel_id=1, source_target_pairs={{0,1},{1,2},{2,3},{3,0},{4,5},{5,6},{6,7},{7,4},{8,9},{9,10},{10,1... | collective-permute-start | bytes 393224 | tf_op jit(solution)/shard_map/ppermute | solution.py:29
  29.6 10.5 %collective-permute-start.6 = (bf16[16,32,128]{2,0,1:T(8,128)(2,1)S(1)}, bf16[16,32,128]{2,0,1:T(8,128)(2,1)S(1)}, u32[]{:S(2)}, u32[]{:S(2)}) collective-permute-start(bf16[16,32,128]{2,0,1:T(8,128)(2,1)S(1)} %fusion.7), channel_id=1, source_target_pairs={{1,0},{2,1},{3,2},{0,3},{5,4},{6,5},{7,6},{4,7},{9,8},{10,9},{11,1... | collective-permute-start | bytes 393224 | tf_op jit(solution)/shard_map/ppermute | solution.py:31
  33.9 6.2 %collective-permute-start.5 = (bf16[16,32,128]{2,0,1:T(8,128)(2,1)S(1)}, bf16[16,32,128]{2,0,1:T(8,128)(2,1)S(1)}, u32[]{:S(2)}, u32[]{:S(2)}) collective-permute-start(bf16[16,32,128]{2,0,1:T(8,128)(2,1)S(1)} %collective-permute-done.4), channel_id=1, source_target_pairs={{0,1},{1,2},{2,3},{3,0},{4,5},{5,6},{6,7},{7,4},{8,9},{9,10},{10,1... | collective-permute-start | bytes 393224 | tf_op jit(solution)/shard_map/ppermute | solution.py:29
  63.6 51.9 %collective-permute-start.7 = (f32[16,32,128]{2,0,1:T(8,128)}, f32[16,32,128]{2,0,1:T(8,128)S(1)}, u32[]{:S(2)}, u32[]{:S(2)}) collective-permute-start(f32[16,32,128]{2,0,1:T(8,128)} %get-tuple-element.18), channel_id=1, source_target_pairs={{8,0},{12,4},{16,8},{20,12},{24,16},{28,20},{0,24},{4,28},{9,1},{1... | collective-permute-start | bytes 786440 | tf_op jit(solution)/shard_map/ppermute | solution.py:41
  66.0 49.5 %collective-permute-start.10 = (f32[16,32,128]{2,0,1:T(8,128)}, f32[16,32,128]{2,0,1:T(8,128)S(1)}, u32[]{:S(2)}, u32[]{:S(2)}) collective-permute-start(f32[16,32,128]{2,0,1:T(8,128)} %get-tuple-element.19), channel_id=1, source_target_pairs={{24,0},{28,4},{0,8},{4,12},{8,16},{12,20},{16,24},{20,28},{25,1},{... | collective-permute-start | bytes 786440 | tf_op jit(solution)/shard_map/ppermute | solution.py:41
  66.0 49.5 %collective-permute-start.9 = (f32[16,32,128]{2,0,1:T(8,128)S(1)}, f32[16,32,128]{2,0,1:T(8,128)S(1)}, u32[]{:S(2)}, u32[]{:S(2)}) collective-permute-start(f32[16,32,128]{2,0,1:T(8,128)S(1)} %get-tuple-element.20), channel_id=1, source_target_pairs={{28,0},{0,4},{4,8},{8,12},{12,16},{16,20},{20,24},{24,28},{29,1},{... | collective-permute-start | bytes 786440 | tf_op jit(solution)/shard_map/ppermute | solution.py:41
  68.9 46.6 %collective-permute-start.8 = (f32[16,32,128]{2,0,1:T(8,128)S(1)}, f32[16,32,128]{2,0,1:T(8,128)S(1)}, u32[]{:S(2)}, u32[]{:S(2)}) collective-permute-start(f32[16,32,128]{2,0,1:T(8,128)S(1)} %get-tuple-element.21), channel_id=1, source_target_pairs={{4,0},{8,4},{12,8},{16,12},{20,16},{24,20},{28,24},{0,28},{5,1},{9... | collective-permute-start | bytes 786440 | tf_op jit(solution)/shard_map/ppermute | solution.py:41
